TPU v7x, 256 devices: a whole 4x4x8 slice. The times are simulated.
256 devices in a mesh: grp: 8 (over z), dev: 32 (over y, x, core).
Axes of the slice: x: 4, y: 4, z: 8, core: 2. Of those that a mesh axis runs over, the one named last changes fastest.
Arguments:
- pool: bfloat16 [786432, 1024], P(('grp', 'dev'))
- nearest: float32 [786432], P(('grp', 'dev')), may hold values from 0.5 to 2.2
- center_owner: int32 [8, 256], P('grp'), may hold values from 0 to 31, as said below
- center_offset: int32 [8, 256], P('grp'), may hold values from 0 to 3071
Outputs:
- nearest_after: float32 [786432], P(('grp', 'dev'))
Inputs may be any that keep to these rules, and one draw needn't show every extreme that they name: `center_owner`: in each group no more than 32 centers have the same owner, one owner has exactly 32, and the centers of a group are distinct rows.
All inputs are finite; a program needn't handle non-finite values.
Results may differ from a plain program's by a relative error of at most 0.0003.
Values may be sent and summed in bfloat16 or wider, within the bound.
No kernel may reach another device: no remote copies, remote signals or barrier semaphores. Data moves between devices by JAX's collectives and lax.ppermute only.
A program may use at most 64 MiB of HBM per device.

v0:
```python
import math
import jax
import jax.numpy as jnp
from jax import lax
from jax.sharding import PartitionSpec as P

MOST = 32


def nearest_fold(pool_rows, row_norm, running, fragment):
    center_norm = jnp.einsum("cd,cd->c", fragment, fragment, preferred_element_type=jnp.float32)
    total_rows = pool_rows.shape[0]
    block = math.gcd(total_rows, 512)
    blocks = total_rows // block

    def one_block(args):
        block_rows, block_norm, block_near = args
        inner = lax.dot_general(
            block_rows, fragment, (((1,), (1,)), ((), ())), preferred_element_type=jnp.float32
        )
        distance = jnp.maximum(block_norm[:, None] + center_norm[None, :] - 2.0 * inner, 0.0)
        return jnp.minimum(block_near, jnp.min(distance, axis=1))

    result = lax.map(
        one_block,
        (
            pool_rows.reshape(blocks, block, pool_rows.shape[1]),
            row_norm.reshape(blocks, block),
            running.reshape(blocks, block),
        ),
    )
    return result.reshape(total_rows)


def shards(pool, nearest, center_owner, center_offset):
    owners = center_owner[0]
    offsets = center_offset[0]
    dev_count = lax.axis_size("dev")
    my_index = lax.axis_index("dev")
    per_device = owners.shape[0] // dev_count
    owner_hot = (owners[:, None] == jnp.arange(dev_count, dtype=jnp.int32)[None, :]).astype(
        jnp.int32
    )
    slot_rank = jnp.sum((jnp.cumsum(owner_hot, axis=0) - 1) * owner_hot, axis=1)
    chosen = (
        (owners == my_index)[None, :]
        & (slot_rank[None, :] == jnp.arange(MOST, dtype=jnp.int32)[:, None])
    ).astype(jnp.int32)
    slot_offsets = jnp.sum(chosen * offsets[None, :], axis=1)
    slot_rows = jnp.take(pool, slot_offsets, axis=0)
    every_slot = lax.all_gather(slot_rows, "dev", axis=0, tiled=True)
    slot_index = owners * MOST + slot_rank
    mine = lax.dynamic_slice_in_dim(slot_index, my_index * per_device, per_device)
    local_centers = jnp.take(every_slot, mine, axis=0)
    row_norm = jnp.einsum("rd,rd->r", pool, pool, preferred_element_type=jnp.float32)
    return nearest_fold(
        pool, row_norm, nearest, lax.all_gather(local_centers, ("grp", "dev"), axis=0, tiled=True)
    )


def solution(mesh):
    in_specs = (P(("grp", "dev"), None), P(("grp", "dev")), P("grp", None), P("grp", None))
    out_specs = P(("grp", "dev"))
    return jax.shard_map(shards, mesh=mesh, in_specs=in_specs, out_specs=out_specs, check_vma=False)
```

profile of v0, /device:TPU:1, one launch (start us, length us, event | category | flops | bytes accessed | tf_op | source)
XLA Modules:
  0.0 228.6 jit_solution(5956748127939711534)
XLA Ops:
  6.5 0.0 copy-start
  6.5 0.0 all-gather.3.cloned.1.call-start
  6.5 0.7 fusion.7
  7.2 0.6 reduce-window.6
  7.8 0.2 slice_reduce_fusion
  8.0 0.7 compare_reduce_fusion
  8.7 0.8 fusion.6
  9.5 0.8 select_reduce_fusion
  10.3 4.3 %gather_fusion = bf16[32,1024]{1,0:T(8,128)(2,1)S(1)} fusion(bf16[3072,1024]{1,0:T(8,128)(2,1)} %param.6, s32[1024]{0:T(1024)S(1)} %pad_clamp_fusion.1), kind=kCustom, calls=%fused_computation | custom fusion | bytes 131200 | tf_op jit(solution)/shard_map/jit(_take)/gather | solution.py:50
  14.6 0.7 broadcast_select_fusion
  15.3 0.0 all-gather.3.cloned.1.call-update
  15.3 0.0 all-gather.5.cloned.1.call-start
  15.4 0.7 multiply_add_fusion
  16.1 0.1 compare_and_fusion.1
  16.2 52.4 %all-gather.3.cloned.1.call-done = bf16[1024,1024]{1,0:T(8,128)(2,1)} async-done(((bf16[32,1024]{1,0:T(8,128)(2,1)}), bf16[1024,1024]{1,0:T(8,128)(2,1)}) %all-gather.3.cloned.1.call-update) | async-done | bytes 2097168 | tf_op jit(solution)/shard_map/all_gather | solution.py:51
  68.6 2.4 %gather_fusion.1 = bf16[8,1024]{1,0:T(8,128)(2,1)S(1)} fusion(bf16[1024,1024]{1,0:T(8,128)(2,1)} %all-gather.3.cloned.1.call-done, s32[1024]{0:T(1024)S(1)} %pad_clamp_fusion), kind=kCustom, calls=%fused_computation.1 | custom fusion | bytes 32800 | tf_op jit(solution)/shard_map/jit(_take)/gather | solution.py:54
  71.0 0.7 broadcast_select_fusion.1
  71.7 0.0 all-gather.5.cloned.1.call-update
  71.7 4.1 %fusion.3 = f32[3072]{0:T(1024)S(1)} fusion(bf16[3072,1024]{1,0:T(8,128)(2,1)} %param.6), kind=kLoop, calls=%fused_computation.9 | loop fusion | flops 9434112 | bytes 6303744 | tf_op jit(solution)/shard_map/rd,rd->r/dot_general | solution.py:55
  75.8 0.0 copy-done
  75.9 110.8 %all-gather.5.cloned.1.call-done = bf16[2048,1024]{1,0:T(8,128)(2,1)} async-done(((bf16[8,1024]{1,0:T(8,128)(2,1)}), bf16[2048,1024]{1,0:T(8,128)(2,1)}) %all-gather.5.cloned.1.call-update) | async-done | bytes 4194320 | tf_op jit(solution)/shard_map/all_gather | solution.py:57
  186.6 3.1 %fusion.4 = f32[2048]{0:T(1024)S(1)} fusion(bf16[2048,1024]{1,0:T(8,128)(2,1)} %all-gather.5.cloned.1.call-done), kind=kLoop, calls=%fused_computation.11 | loop fusion | flops 6289408 | bytes 4202496 | tf_op jit(solution)/shard_map/cd,cd->c/dot_general | solution.py:11
  189.7 31.4 %while.10 = (s32[]{:T(128)}, f32[6,512]{1,0:T(8,128)S(1)}, f32[6,512]{1,0:T(8,128)S(1)}, f32[6,512]{1,0:T(8,128)S(1)}, f32[2048]{0:T(1024)S(1)}, /*index=5*/bf16...) while((s32[]{:T(128)}, f32[6,512]{1,0:T(8,128)S(1)}, f32[6,512]{1,0:T(8,128)S(1)}, ...), condition=%wide.region_6.7_spmd, body=%wide.region_4.6_spmd.sunk | while | flops 2152726528 | bytes 5270121 | solution.py:24
  189.7 5.1 %maximum_reduce_fusion.2 = f32[512]{0:T(512)S(1)} fusion(bf16[2048,1024]{1,0:T(8,128)(2,1)} %get-tuple-element.126, f32[2048]{0:T(1024)S(1)} %get-tuple-element.124, f32[512]{0:T(512)S(1)} %bitcast.39, bf16[6,512,1024]{2,1,0:T(8,128)(2,1)} %get-tuple-element.125, s32[]{:T(128)} %get-tuple-element.111), kind=kOutput, calls=%fused_computation.2.clone.1 | convolution fusion | flops 2152726016 | bytes 5255680 | tf_op jit(solution)/shard_map/while/body/eval_jaxpr/dot_general | solution.py:18
  194.9 0.1 dynamic_update_slice.5
  195.0 5.1 %maximum_reduce_fusion.2 = f32[512]{0:T(512)S(1)} fusion(bf16[2048,1024]{1,0:T(8,128)(2,1)} %get-tuple-element.126, f32[2048]{0:T(1024)S(1)} %get-tuple-element.124, f32[512]{0:T(512)S(1)} %bitcast.39, bf16[6,512,1024]{2,1,0:T(8,128)(2,1)} %get-tuple-element.125, s32[]{:T(128)} %get-tuple-element.111), kind=kOutput, calls=%fused_computation.2.clone.1 | convolution fusion | flops 2152726016 | bytes 5255680 | tf_op jit(solution)/shard_map/while/body/eval_jaxpr/dot_general | solution.py:18
  200.1 0.1 dynamic_update_slice.5
  200.2 5.1 %maximum_reduce_fusion.2 = f32[512]{0:T(512)S(1)} fusion(bf16[2048,1024]{1,0:T(8,128)(2,1)} %get-tuple-element.126, f32[2048]{0:T(1024)S(1)} %get-tuple-element.124, f32[512]{0:T(512)S(1)} %bitcast.39, bf16[6,512,1024]{2,1,0:T(8,128)(2,1)} %get-tuple-element.125, s32[]{:T(128)} %get-tuple-element.111), kind=kOutput, calls=%fused_computation.2.clone.1 | convolution fusion | flops 2152726016 | bytes 5255680 | tf_op jit(solution)/shard_map/while/body/eval_jaxpr/dot_general | solution.py:18
  205.3 0.1 dynamic_update_slice.5
  205.4 5.1 %maximum_reduce_fusion.2 = f32[512]{0:T(512)S(1)} fusion(bf16[2048,1024]{1,0:T(8,128)(2,1)} %get-tuple-element.126, f32[2048]{0:T(1024)S(1)} %get-tuple-element.124, f32[512]{0:T(512)S(1)} %bitcast.39, bf16[6,512,1024]{2,1,0:T(8,128)(2,1)} %get-tuple-element.125, s32[]{:T(128)} %get-tuple-element.111), kind=kOutput, calls=%fused_computation.2.clone.1 | convolution fusion | flops 2152726016 | bytes 5255680 | tf_op jit(solution)/shard_map/while/body/eval_jaxpr/dot_general | solution.py:18
  210.6 0.1 dynamic_update_slice.5
  210.7 5.1 %maximum_reduce_fusion.2 = f32[512]{0:T(512)S(1)} fusion(bf16[2048,1024]{1,0:T(8,128)(2,1)} %get-tuple-element.126, f32[2048]{0:T(1024)S(1)} %get-tuple-element.124, f32[512]{0:T(512)S(1)} %bitcast.39, bf16[6,512,1024]{2,1,0:T(8,128)(2,1)} %get-tuple-element.125, s32[]{:T(128)} %get-tuple-element.111), kind=kOutput, calls=%fused_computation.2.clone.1 | convolution fusion | flops 2152726016 | bytes 5255680 | tf_op jit(solution)/shard_map/while/body/eval_jaxpr/dot_general | solution.py:18
  215.8 0.1 dynamic_update_slice.5
  215.9 5.1 %maximum_reduce_fusion.2 = f32[512]{0:T(512)S(1)} fusion(bf16[2048,1024]{1,0:T(8,128)(2,1)} %get-tuple-element.126, f32[2048]{0:T(1024)S(1)} %get-tuple-element.124, f32[512]{0:T(512)S(1)} %bitcast.39, bf16[6,512,1024]{2,1,0:T(8,128)(2,1)} %get-tuple-element.125, s32[]{:T(128)} %get-tuple-element.111), kind=kOutput, calls=%fused_computation.2.clone.1 | convolution fusion | flops 2152726016 | bytes 5255680 | tf_op jit(solution)/shard_map/while/body/eval_jaxpr/dot_general | solution.py:18
  221.0 0.1 dynamic_update_slice.5
  221.1 0.6 reshape.63
  (21 shorter events, 0.2 us)
Async XLA Ops:
  6.5 69.3 %copy-start = (f32[3072]{0:T(1024)S(1)}, f32[3072]{0:T(1024)}, u32[]{:S(2)}) copy-start(f32[3072]{0:T(1024)} %param.7) | copy-start | bytes 36868
  6.5 62.0 %all-gather.3.cloned.1.call-start = ((), (), s32[]{:S(2)}) async-start(), calls=%async_computation | async-start | bytes 2162688 | tf_op jit(solution)/shard_map/all_gather | solution.py:51
  15.3 171.3 %all-gather.5.cloned.1.call-start = ((), (), s32[]{:S(2)}) async-start(), calls=%async_computation.1 | async-start | bytes 4210688 | tf_op jit(solution)/shard_map/all_gather | solution.py:57
Sparse Core Ops, SparseCore 0:
  15.5 53.0 all-gather.2
  72.2 114.3 all-gather.4
where the time goes:
time: 229 us
  waiting for transfers between devices  163 us (71%)
  matrix products  30.7 us (13%)
  between operations  13.5 us (6%)
  other arithmetic  13 us (6%)
  local copies, waits for them, and re-layouts  7.93 us (3%)
    all_gather x1, waiting for transfers between devices, shards(): lax.all_gather(local_centers, ('grp', 'dev'), axis=0, tiled=True)  111 us
    all_gather x1, waiting for transfers between devices, shards(): every_slot = lax.all_gather(slot_rows, 'dev', axis=0, tiled=True)  52.4 us
    dot_general x6, matrix products, one_block(): lax.dot_general(block_rows, fragment, (((1,), (1,)), ((), ())), preferred...  30.7 us
  transfers between devices with their start and end apart: 2, of which 2 were waited for; matrix products, arithmetic and copies ran while one was open for 2% of the time, Pallas kernels for 0%

commit v1 on v0

--- a/solution.py
+++ b/solution.py
@@ -48,7 +48,9 @@
     ).astype(jnp.int32)
     slot_offsets = jnp.sum(chosen * offsets[None, :], axis=1)
     slot_rows = jnp.take(pool, slot_offsets, axis=0)
-    every_slot = lax.all_gather(slot_rows, "dev", axis=0, tiled=True)
+    every_slot = jnp.concatenate(
+        lax.all_to_all(jnp.stack([slot_rows] * lax.axis_size("dev")), "dev", 0, 0), axis=0
+    )
     slot_index = owners * MOST + slot_rank
     mine = lax.dynamic_slice_in_dim(slot_index, my_index * per_device, per_device)
     local_centers = jnp.take(every_slot, mine, axis=0)

time: 229 us -> 213 us (0.930)
  waiting for transfers between devices: 163 us -> 140 us
  starting transfers between devices: 0.04 us -> 8.63 us
    all_gather x1 -> x0, waiting for transfers between devices: 52.4 us -> none  [shards(): every_slot = lax.all_gather(slot_rows, 'dev', axis=0, tiled=True)]
    all_to_all x0 -> x1, waiting for transfers between devices: none -> 27.7 us  [shards(): lax.all_to_all(jnp.stack([slot_rows] * lax.axis_size('dev')), 'dev', 0, 0)]
    all_to_all x0 -> x1, starting transfers between devices: none -> 8.59 us  [shards(): lax.all_to_all(jnp.stack([slot_rows] * lax.axis_size('dev')), 'dev', 0, 0)]
where the time goes in v1:
time: 213 us; the launch traced here: 212 us
  waiting for transfers between devices  140 us (66%)
  matrix products  30.7 us (14%)
  between operations  13.5 us (6%)
  other arithmetic  11.7 us (5%)
  starting transfers between devices  8.63 us (4%)
  local copies, waits for them, and re-layouts  7.68 us (4%)
    all_gather x1, waiting for transfers between devices, shards(): lax.all_gather(local_centers, ('grp', 'dev'), axis=0, tiled=True)  112 us
    dot_general x6, matrix products, one_block(): lax.dot_general(block_rows, fragment, (((1,), (1,)), ((), ())), preferred...  30.7 us
    all_to_all x1, waiting for transfers between devices, shards(): lax.all_to_all(jnp.stack([slot_rows] * lax.axis_size('dev')), 'dev', 0, 0)  27.7 us
    all_to_all x1, starting transfers between devices, shards(): lax.all_to_all(jnp.stack([slot_rows] * lax.axis_size('dev')), 'dev', 0, 0)  8.59 us
    gather x1, local copies, waits for them, and re-layouts, shards(): slot_rows = jnp.take(pool, slot_offsets, axis=0)  4.27 us
  transfers between devices with their start and end apart: 2, of which 2 were waited for; matrix products, arithmetic and copies ran while one was open for 2% of the time, Pallas kernels for 0%

profile of v1, /device:TPU:1, one launch (start us, length us, event | category | flops | bytes accessed | tf_op | source)
XLA Modules:
  0.0 212.2 jit_solution(14937177414396744674)
XLA Ops:
  6.5 0.0 copy-start
  6.5 0.8 fusion.7
  7.3 0.6 reduce-window.6
  7.9 0.2 slice_reduce_fusion
  8.1 0.7 compare_reduce_fusion
  8.8 0.8 fusion.6
  9.6 0.8 select_reduce_fusion
  10.4 4.3 %gather_fusion = bf16[32,1024]{1,0:T(8,128)(2,1)S(1)} fusion(bf16[3072,1024]{1,0:T(8,128)(2,1)} %param.6, s32[1024]{0:T(1024)S(1)} %pad_clamp_fusion.1), kind=kCustom, calls=%fused_computation | custom fusion | bytes 131200 | tf_op jit(solution)/shard_map/jit(_take)/gather | solution.py:50
  14.7 0.1 broadcast_select_fusion
  14.8 1.6 stack.2
  16.4 8.6 %all-to-all-start = ((bf16[32,32,1024]{2,1,0:T(8,128)(2,1)}), bf16[32,32,1024]{2,1,0:T(8,128)(2,1)S(1)}, u32[]{:S(2)}, u32[]{:S(2)}) async-start(bf16[32,32,1024]{2,1,0:T(8,128)(2,1)} %stack.2), calls=%async_computation | async-start | bytes 4194304 | tf_op jit(solution)/shard_map/all_to_all | solution.py:52
  25.0 0.0 copy-start.1
  25.0 0.0 all-gather.2.cloned.1.call-start
  25.0 0.0 copy-done
  25.1 0.1 compare_and_fusion.1
  25.1 27.7 %all-to-all-done = bf16[32,32,1024]{2,1,0:T(8,128)(2,1)S(1)} async-done(((bf16[32,32,1024]{2,1,0:T(8,128)(2,1)}), bf16[32,32,1024]{2,1,0:T(8,128)(2,1)S(1)}, u32[]{:S(2)}, u32[]{:S(2)}) %all-to-all-start) | async-done | bytes 2097184 | tf_op jit(solution)/shard_map/all_to_all | solution.py:52
  52.8 0.6 gather_fusion.1
  53.4 0.7 broadcast_select_fusion.1
  54.1 0.0 all-gather.2.cloned.1.call-update
  54.1 4.1 %fusion.3 = f32[3072]{0:T(1024)S(1)} fusion(bf16[3072,1024]{1,0:T(8,128)(2,1)} %param.6), kind=kLoop, calls=%fused_computation.9 | loop fusion | flops 9434112 | bytes 6303744 | tf_op jit(solution)/shard_map/rd,rd->r/dot_general | solution.py:57
  58.2 0.0 copy-done.1
  58.2 112.0 %all-gather.2.cloned.1.call-done = bf16[2048,1024]{1,0:T(8,128)(2,1)} async-done(((bf16[8,1024]{1,0:T(8,128)(2,1)}), bf16[2048,1024]{1,0:T(8,128)(2,1)}) %all-gather.2.cloned.1.call-update) | async-done | bytes 4194320 | tf_op jit(solution)/shard_map/all_gather | solution.py:59
  170.2 3.1 %fusion.4 = f32[2048]{0:T(1024)S(1)} fusion(bf16[2048,1024]{1,0:T(8,128)(2,1)} %all-gather.2.cloned.1.call-done), kind=kLoop, calls=%fused_computation.11 | loop fusion | flops 6289408 | bytes 4202496 | tf_op jit(solution)/shard_map/cd,cd->c/dot_general | solution.py:11
  173.3 31.4 %while.10 = (s32[]{:T(128)}, f32[6,512]{1,0:T(8,128)S(1)}, f32[6,512]{1,0:T(8,128)S(1)}, f32[6,512]{1,0:T(8,128)S(1)}, f32[2048]{0:T(1024)S(1)}, /*index=5*/bf16...) while((s32[]{:T(128)}, f32[6,512]{1,0:T(8,128)S(1)}, f32[6,512]{1,0:T(8,128)S(1)}, ...), condition=%wide.region_6.7_spmd, body=%wide.region_4.6_spmd.sunk | while | flops 2152726528 | bytes 5270121 | solution.py:24
  173.3 5.1 %maximum_reduce_fusion.2 = f32[512]{0:T(512)S(1)} fusion(bf16[2048,1024]{1,0:T(8,128)(2,1)} %get-tuple-element.126, f32[2048]{0:T(1024)S(1)} %get-tuple-element.124, f32[512]{0:T(512)S(1)} %bitcast.41, bf16[6,512,1024]{2,1,0:T(8,128)(2,1)} %get-tuple-element.125, s32[]{:T(128)} %get-tuple-element.111), kind=kOutput, calls=%fused_computation.2.clone.1 | convolution fusion | flops 2152726016 | bytes 5255680 | tf_op jit(solution)/shard_map/while/body/eval_jaxpr/dot_general | solution.py:18
  178.5 0.1 dynamic_update_slice.5
  178.6 5.1 %maximum_reduce_fusion.2 = f32[512]{0:T(512)S(1)} fusion(bf16[2048,1024]{1,0:T(8,128)(2,1)} %get-tuple-element.126, f32[2048]{0:T(1024)S(1)} %get-tuple-element.124, f32[512]{0:T(512)S(1)} %bitcast.41, bf16[6,512,1024]{2,1,0:T(8,128)(2,1)} %get-tuple-element.125, s32[]{:T(128)} %get-tuple-element.111), kind=kOutput, calls=%fused_computation.2.clone.1 | convolution fusion | flops 2152726016 | bytes 5255680 | tf_op jit(solution)/shard_map/while/body/eval_jaxpr/dot_general | solution.py:18
  183.7 0.1 dynamic_update_slice.5
  183.8 5.1 %maximum_reduce_fusion.2 = f32[512]{0:T(512)S(1)} fusion(bf16[2048,1024]{1,0:T(8,128)(2,1)} %get-tuple-element.126, f32[2048]{0:T(1024)S(1)} %get-tuple-element.124, f32[512]{0:T(512)S(1)} %bitcast.41, bf16[6,512,1024]{2,1,0:T(8,128)(2,1)} %get-tuple-element.125, s32[]{:T(128)} %get-tuple-element.111), kind=kOutput, calls=%fused_computation.2.clone.1 | convolution fusion | flops 2152726016 | bytes 5255680 | tf_op jit(solution)/shard_map/while/body/eval_jaxpr/dot_general | solution.py:18
  188.9 0.1 dynamic_update_slice.5
  189.0 5.1 %maximum_reduce_fusion.2 = f32[512]{0:T(512)S(1)} fusion(bf16[2048,1024]{1,0:T(8,128)(2,1)} %get-tuple-element.126, f32[2048]{0:T(1024)S(1)} %get-tuple-element.124, f32[512]{0:T(512)S(1)} %bitcast.41, bf16[6,512,1024]{2,1,0:T(8,128)(2,1)} %get-tuple-element.125, s32[]{:T(128)} %get-tuple-element.111), kind=kOutput, calls=%fused_computation.2.clone.1 | convolution fusion | flops 2152726016 | bytes 5255680 | tf_op jit(solution)/shard_map/while/body/eval_jaxpr/dot_general | solution.py:18
  194.2 0.1 dynamic_update_slice.5
  194.3 5.1 %maximum_reduce_fusion.2 = f32[512]{0:T(512)S(1)} fusion(bf16[2048,1024]{1,0:T(8,128)(2,1)} %get-tuple-element.126, f32[2048]{0:T(1024)S(1)} %get-tuple-element.124, f32[512]{0:T(512)S(1)} %bitcast.41, bf16[6,512,1024]{2,1,0:T(8,128)(2,1)} %get-tuple-element.125, s32[]{:T(128)} %get-tuple-element.111), kind=kOutput, calls=%fused_computation.2.clone.1 | convolution fusion | flops 2152726016 | bytes 5255680 | tf_op jit(solution)/shard_map/while/body/eval_jaxpr/dot_general | solution.py:18
  199.4 0.1 dynamic_update_slice.5
  199.5 5.1 %maximum_reduce_fusion.2 = f32[512]{0:T(512)S(1)} fusion(bf16[2048,1024]{1,0:T(8,128)(2,1)} %get-tuple-element.126, f32[2048]{0:T(1024)S(1)} %get-tuple-element.124, f32[512]{0:T(512)S(1)} %bitcast.41, bf16[6,512,1024]{2,1,0:T(8,128)(2,1)} %get-tuple-element.125, s32[]{:T(128)} %get-tuple-element.111), kind=kOutput, calls=%fused_computation.2.clone.1 | convolution fusion | flops 2152726016 | bytes 5255680 | tf_op jit(solution)/shard_map/while/body/eval_jaxpr/dot_general | solution.py:18
  204.7 0.1 dynamic_update_slice.5
  204.7 0.6 reshape.74
  (22 shorter events, 0.2 us)
Async XLA Ops:
  6.5 18.5 %copy-start = (s32[1,256]{1,0:T(1,128)S(1)}, s32[1,256]{1,0:T(1,128)}, u32[]{:S(2)}) copy-start(s32[1,256]{1,0:T(1,128)} %param.8) | copy-start | bytes 3076
  16.4 36.4 %all-to-all-start = ((bf16[32,32,1024]{2,1,0:T(8,128)(2,1)}), bf16[32,32,1024]{2,1,0:T(8,128)(2,1)S(1)}, u32[]{:S(2)}, u32[]{:S(2)}) async-start(bf16[32,32,1024]{2,1,0:T(8,128)(2,1)} %stack.2), calls=%async_computation | async-start | bytes 4194304 | tf_op jit(solution)/shard_map/all_to_all | solution.py:52
  25.0 33.2 %copy-start.1 = (f32[3072]{0:T(1024)S(1)}, f32[3072]{0:T(1024)}, u32[]{:S(2)}) copy-start(f32[3072]{0:T(1024)} %param.7) | copy-start | bytes 36868
  25.0 145.2 %all-gather.2.cloned.1.call-start = ((), (), s32[]{:S(2)}) async-start(), calls=%async_computation.1 | async-start | bytes 4210688 | tf_op jit(solution)/shard_map/all_gather | solution.py:59
Sparse Core Ops, SparseCore 0:
  54.2 115.9 all-gather.1
